TPU v7x, 32 devices: a whole 2x2x4 slice. The times are simulated.
32 devices in a mesh: groups: 2 (over y), wide: 4 (over z), ctx: 4 (over x, core).
Axes of the slice: x: 2, y: 2, z: 4, core: 2. Of those that a mesh axis runs over, the one named last changes fastest.
Arguments:
- queries: bfloat16 [4096, 6144], P(('groups', 'ctx'), 'wide'), parts along dimension 0, may hold values from -48 to 48
- key_rows: bfloat16 [4096, 1024], P(('groups', 'ctx')), parts along dimension 0, may hold values from -48 to 48
- value_head_rows: bfloat16 [4096, 1024], P(('groups', 'ctx')), parts along dimension 0, may hold values from -18 to 18
- residual: bfloat16 [4096, 6144], P(('groups', 'ctx'), 'wide'), parts along dimension 0, may hold values from -48 to 48
- out_weight: bfloat16 [6144, 6144], P('wide'), may hold values from -0.109375 to 0.109375
- norm_gain: bfloat16 [6144], P('wide'), may hold values from 0.25 to 1.75
- router_weight: bfloat16 [6144, 8], P('wide'), may hold values from -0.078125 to 0.078125
- gate_weight: bfloat16 [6144, 8192], P('wide', 'ctx'), may hold values from -0.078125 to 0.078125
- up_weight: bfloat16 [6144, 8192], P('wide', 'ctx'), may hold values from -0.078125 to 0.078125
- down_weight: bfloat16 [8192, 6144], P('ctx', 'wide'), may hold values from -0.0625 to 0.0625
- expert_ids: int32 [4096, 2], P('groups'), parts along dimension 0, may hold values from 0 to 7, as said below
- slot_ids: int32 [4096, 2], P('groups'), parts along dimension 0, may hold values from -1 to 639, as said below
Outputs:
- layer_out: bfloat16 [4096, 6144], P(('groups', 'ctx'), 'wide'), parts along dimension 0
There are 2 independent parts, one for each index of `groups`. A program takes and returns all parts, laid end to end along the dimension named above; an argument that names none is the same for every part. Nothing has to cross between parts.
Inputs may be any that keep to these rules, and one draw needn't show every extreme that they name: `expert_ids`: each row names 2 different experts; expert 0 is named by at least 704 rows, so its buffer is full in every draw. `slot_ids`: the rows naming one expert take its buffer rows 0, 1, 2 and so on in the order of positions (for one position, the earlier column first); once 640 rows are taken, further choices of that expert hold -1. Rows of one expert's buffer are never shared.
All inputs are finite; a program needn't handle non-finite values.
Results may differ from a plain program's by a relative error of at most 0.015.
Values may be sent and summed in bfloat16 or wider, within the bound.
No kernel may reach another device: no remote copies, remote signals or barrier semaphores. Data moves between devices by JAX's collectives and lax.ppermute only.
A program may use at most 192 MiB of HBM per device.

v0:
```python
import math
import jax
import jax.numpy as jnp
from jax import lax
from jax.sharding import PartitionSpec as P

D = 6144
QUERY_HEADS = 48
KEY_VALUE_HEADS = 8
HEAD_SIZE = 128
NEG_FILL = -1e30
EPSILON = 1e-05


def token_slots(expert_ids, slot_ids, capacity):
    in_window = jnp.logical_and(expert_ids == 0, slot_ids >= 0)
    picked = jnp.max(jnp.where(in_window, slot_ids, -1), axis=1)
    return jnp.where(picked >= 0, picked, capacity)


def other_experts(expert_ids, slot_of_token, capacity):
    partner = jnp.sum(expert_ids, axis=1)
    return jnp.zeros((capacity,), jnp.int32).at[slot_of_token].set(partner, mode="drop")


def expert_hidden(gate_sum, up_sum, square_sum, logit_sum, slot_other, model_width):
    inverse_rms = lax.rsqrt(square_sum / model_width + EPSILON)
    gate_value = gate_sum * inverse_rms[:, None]
    up_value = up_sum * inverse_rms[:, None]
    logit_value = logit_sum * inverse_rms[:, None]
    columns = jnp.arange(logit_value.shape[1], dtype=jnp.int32)
    partner_logit = jnp.sum(
        jnp.where(columns[None, :] == slot_other[:, None], logit_value, 0.0), axis=1
    )
    mixing = jax.nn.sigmoid(logit_value[:, 0] - partner_logit)
    return (jax.nn.silu(gate_value) * up_value * mixing[:, None]).astype(jnp.bfloat16)


def local(
    queries,
    key_rows,
    value_head_rows,
    residual,
    out_weight,
    norm_gain,
    router_weight,
    gate_weight,
    up_weight,
    down_weight,
    expert_ids,
    slot_ids,
):
    ctx_count = lax.axis_size("ctx")
    wide_index = lax.axis_index("wide")
    ctx_index = lax.axis_index("ctx")
    rows_local = queries.shape[0]
    heads_local = queries.shape[1] // HEAD_SIZE
    query_group_width = QUERY_HEADS // KEY_VALUE_HEADS
    shared_heads = max(1, heads_local // query_group_width)
    per_shared = heads_local // shared_heads
    first_shared = wide_index * heads_local // query_group_width
    key_used = lax.dynamic_slice_in_dim(
        key_rows, first_shared * HEAD_SIZE, shared_heads * HEAD_SIZE, 1
    )
    value_used = lax.dynamic_slice_in_dim(
        value_head_rows, first_shared * HEAD_SIZE, shared_heads * HEAD_SIZE, 1
    )
    query_blocks = queries.reshape(rows_local, shared_heads, per_shared, HEAD_SIZE)
    query_pos = ctx_index * rows_local + jnp.arange(rows_local, dtype=jnp.int32)
    last_query = ctx_index * rows_local + rows_local - 1
    scale_factor = 1.0 / math.sqrt(HEAD_SIZE)
    start_state = (
        jnp.full((shared_heads, per_shared, rows_local), -jnp.inf, jnp.float32),
        jnp.zeros((shared_heads, per_shared, rows_local), jnp.float32),
        jnp.zeros((shared_heads, per_shared, rows_local, HEAD_SIZE), jnp.float32),
    )
    pieces = (
        lax.all_gather(key_used, "ctx", axis=0, tiled=True),
        lax.all_gather(value_used, "ctx", axis=0, tiled=True),
    )

    def update(state):
        running_max, running_sum, running_acc = state
        key_piece = pieces[0].reshape(-1, shared_heads, HEAD_SIZE)
        value_piece = pieces[1].reshape(-1, shared_heads, HEAD_SIZE)
        scores = (
            jnp.einsum(
                "skqd,rkd->kqsr", query_blocks, key_piece, preferred_element_type=jnp.float32
            )
            * scale_factor
        )
        key_pos = jnp.arange(key_piece.shape[0], dtype=jnp.int32)
        allowed = (key_pos[None, :] <= query_pos[:, None])[None, None, :, :]
        masked = jnp.where(allowed, scores, NEG_FILL)
        new_max = jnp.max(masked, axis=-1)
        weights = jnp.where(allowed, jnp.exp(masked - new_max[..., None]), 0.0)
        decay = jnp.exp(running_max - new_max)
        new_sum = running_sum * decay + jnp.sum(weights, axis=-1)
        added = jnp.einsum(
            "kqsr,rkd->kqsd",
            weights.astype(jnp.bfloat16),
            value_piece,
            preferred_element_type=jnp.float32,
        )
        return (new_max, new_sum, running_acc * decay[..., None] + added)

    final_max, final_sum, final_acc = lax.cond(
        jnp.int32(0) > last_query, lambda state: state, update, start_state
    )
    attended = final_acc / final_sum[..., None]
    attended = (
        jnp.transpose(attended, (2, 0, 1, 3))
        .reshape(rows_local, heads_local * HEAD_SIZE)
        .astype(jnp.bfloat16)
    )
    partial_out = jnp.dot(attended, out_weight, preferred_element_type=jnp.float32)
    head_sum = lax.psum_scatter(
        partial_out.astype(jnp.bfloat16), "wide", scatter_dimension=1, tiled=True
    ).astype(jnp.float32)
    resid = (residual.astype(jnp.float32) + head_sum).astype(jnp.bfloat16)
    seq_len = rows_local * ctx_count
    capacity = seq_len * 5 // 16
    width_local = resid.shape[1]
    slot_of_token = token_slots(expert_ids, slot_ids, capacity)
    slot_other = other_experts(expert_ids, slot_of_token, capacity)
    buffer = (
        jnp.zeros((capacity, width_local), jnp.bfloat16)
        .at[slot_of_token]
        .set(lax.all_gather(resid, "ctx", axis=0, tiled=True), mode="drop")
    )
    buffer_wide = buffer.astype(jnp.float32)
    square_part = jnp.sum(buffer_wide * buffer_wide, axis=1)
    scaled = (buffer_wide * norm_gain.astype(jnp.float32)[None, :]).astype(jnp.bfloat16)
    gate_part = jnp.dot(scaled, gate_weight, preferred_element_type=jnp.float32)
    up_part = jnp.dot(scaled, up_weight, preferred_element_type=jnp.float32)
    logit_part = jnp.dot(scaled, router_weight, preferred_element_type=jnp.float32)
    gate_sum, up_sum, square_sum, logit_sum = (
        lax.psum(gate_part.astype(jnp.bfloat16), "wide").astype(jnp.float32),
        lax.psum(up_part.astype(jnp.bfloat16), "wide").astype(jnp.float32),
        lax.psum(square_part.astype(jnp.bfloat16), "wide").astype(jnp.float32),
        lax.psum(logit_part.astype(jnp.bfloat16), "wide").astype(jnp.float32),
    )
    hidden = expert_hidden(gate_sum, up_sum, square_sum, logit_sum, slot_other, D)
    expert_part = jnp.dot(hidden, down_weight, preferred_element_type=jnp.float32)
    expert_pad = jnp.concatenate([expert_part, jnp.zeros((1, width_local), jnp.float32)], axis=0)
    moe_rows = lax.psum_scatter(
        jnp.take(expert_pad, slot_of_token, axis=0).astype(jnp.bfloat16),
        "ctx",
        scatter_dimension=0,
        tiled=True,
    ).astype(jnp.float32)
    return (resid.astype(jnp.float32) + moe_rows).astype(jnp.bfloat16)


def solution(mesh):
    placed = (
        P(("groups", "ctx"), "wide"),
        P(("groups", "ctx"), None),
        P(("groups", "ctx"), None),
        P(("groups", "ctx"), "wide"),
        P("wide", None),
        P("wide"),
        P("wide", None),
        P("wide", "ctx"),
        P("wide", "ctx"),
        P("ctx", "wide"),
        P("groups", None),
        P("groups", None),
    )
    return jax.shard_map(
        local, mesh=mesh, in_specs=placed, out_specs=P(("groups", "ctx"), "wide"), check_vma=False
    )
```

profile of v0, /device:TPU:0, one launch (start us, length us, event | category | flops | bytes accessed | tf_op | source)
XLA Modules:
  0.0 613.0 jit_solution(8369827461181199514)
XLA Ops:
  6.5 0.0 copy-start
  6.5 0.0 all-gather.4.cloned.1.call-start
  6.5 1.2 copy-done
  7.8 0.7 constant_dynamic-slice_fusion.1
  8.5 0.0 all-gather.4.cloned.1.call-update
  8.5 0.0 all-gather.6.cloned.1.call-start
  8.6 1.7 constant_dynamic-slice_fusion
  10.2 0.0 all-gather.6.cloned.1.call-update
  10.3 0.0 reduce-scatter.3.cloned.1.call-start
  10.3 18.0 %all-gather.4.cloned.1.call-done = bf16[2048,256]{1,0:T(8,128)(2,1)} async-done(((bf16[512,256]{1,0:T(8,128)(2,1)}), bf16[2048,256]{1,0:T(8,128)(2,1)}) %all-gather.4.cloned.1.call-update) | async-done | bytes 1048592 | tf_op jit(solution)/shard_map/all_gather | solution.py:78
  28.3 18.3 %all-gather.6.cloned.1.call-done = bf16[2048,256]{1,0:T(8,128)(2,1)} async-done(((bf16[512,256]{1,0:T(8,128)(2,1)}), bf16[2048,256]{1,0:T(8,128)(2,1)}) %all-gather.6.cloned.1.call-update) | async-done | bytes 1048592 | tf_op jit(solution)/shard_map/all_gather | solution.py:79
  46.6 75.7 %conditional.1 = (f32[2,6,512]{2,1,0:T(8,128)S(1)}, f32[2,6,512,128]{2,3,1,0:T(8,128)}) conditional(s32[]{:T(128)} %convert_element_type.76, (s32[]{:T(128)}, s32[512]{0:T(512)S(1)}, bf16[2048,256]{1,0:T(8,128)(2,1)}, bf16[512,1536]{1,0:T(8,128)(2,1)}, bf16[2048,256]{1,0:T(8,128)(2,1)}) %tuple.13, () %tuple.14), branch_computations={%region_0.3_spmd, %region_3.4_spmd} | conditional | flops 6607870464 | bytes 180058160 | solution.py:107
  46.6 0.8 iota_compare_fusion
  47.5 1.7 copy.28
  49.2 2.1 reshape.71
  51.3 21.1 %fusion = (f32[2,6,512]{2,1,0:T(8,128)S(1)}, f32[2,2048,512,6]{2,1,3,0:T(8,128)}) fusion(pred[512,2048]{0,1:T(8,128)(4,1)S(1)} %iota_compare_fusion, bf16[512,2,6,128]{0,3,2,1:T(8,128)(2,1)S(1)} %bitcast.29, bf16[2048,2,128,1]{2,1,0,3:T(2,128)(2,1)} %bitcast.30), kind=kOutput, calls=%fused_computation.5 | convolution fusion | flops 3258968064 | bytes 54026240 | tf_op jit(solution)/shard_map/cond/branch_0_fun/skqd,rkd->kqsr/dot_general | solution.py:87
  72.4 0.0 copy-start.4
  72.4 22.0 %fusion.2 = f32[2,6,512]{2,1,0:T(8,128)S(1)} fusion(f32[2,2048,512,6]{2,1,3,0:T(8,128)} %get-tuple-element.49, f32[2,6,512]{2,1,0:T(8,128)S(1)} %get-tuple-element.48, pred[512,2048]{0,1:T(8,128)(4,1)S(1)} %iota_compare_fusion), kind=kLoop, calls=%fused_computation.7 | loop fusion | flops 62908416 | bytes 51429376 | tf_op jit(solution)/shard_map/cond/branch_0_fun/reduce_sum | solution.py:98
  94.4 0.0 copy-done.4
  94.4 0.3 reshape.73
  94.7 24.0 %fusion.6 = f32[2,6,512,128]{3,2,1,0:T(8,128)} fusion(f32[2,2048,512,6]{2,1,3,0:T(8,128)} %get-tuple-element.49, f32[2,6,512]{2,1,0:T(8,128)S(1)} %get-tuple-element.48, pred[512,2048]{0,1:T(8,128)(4,1)S(1)} %iota_compare_fusion, f32[2,6,512]{2,1,0:T(8,128)S(1)} %get-tuple-element.46, bf16[2048,2,128,1]{2,1,0,3:T(2,128)(2,1)S(1)} %bitcast.32), kind=kOutput, calls=%fused_computation.11 | convolution fusion | flops 3284926464 | bytes 55623680 | tf_op jit(solution)/shard_map/cond/branch_0_fun/kqsr,rkd->kqsd/dot_general | solution.py:99
  118.8 3.5 copy.38
  122.3 2.3 divide_convert_fusion
  124.7 15.7 %convolution_convert_fusion = bf16[512,6144]{1,0:T(8,128)(2,1)} fusion(bf16[512,1536]{0,1:T(8,128)(2,1)S(1)} %bitcast.31, bf16[1536,6144]{1,0:T(8,128)(2,1)} %param.18), kind=kOutput, calls=%fused_computation.22 | convolution fusion | flops 9666822144 | bytes 26738688 | tf_op jit(solution)/shard_map/dot_general | solution.py:116
  140.3 0.0 copy-start.3
  140.3 0.0 reduce-scatter.3.cloned.1.call-update
  140.4 0.0 copy-start.7
  140.4 0.0 copy-start.5
  140.4 0.0 copy-start.6
  140.4 0.0 all-gather.8.cloned.1.call-start
  140.5 110.8 %reduce-scatter.3.cloned.1.call-done = bf16[512,1536]{1,0:T(8,128)(2,1)} async-done(((bf16[512,6144]{1,0:T(8,128)(2,1)}), bf16[512,1536]{1,0:T(8,128)(2,1)}) %reduce-scatter.3.cloned.1.call-update) | async-done | bytes 1572880 | tf_op jit(solution)/shard_map/reduce_scatter | solution.py:117
  251.3 0.0 copy-done.3
  251.3 2.9 add_convert_fusion.1
  254.2 0.0 all-gather.8.cloned.1.call-update
  254.3 0.0 all-reduce.5.cloned.1.call-start
  254.3 0.0 copy-done.7
  254.3 0.0 copy-done.5
  254.3 0.0 copy-done.6
  254.4 0.1 fusion.33
  254.4 46.9 %all-gather.8.cloned.1.call-done = bf16[2048,1536]{1,0:T(8,128)(2,1)} async-done(((bf16[512,1536]{1,0:T(8,128)(2,1)}), bf16[2048,1536]{1,0:T(8,128)(2,1)}) %all-gather.8.cloned.1.call-update) | async-done | bytes 6291472 | tf_op jit(solution)/shard_map/all_gather | solution.py:129
  301.3 11.4 %scatter_custom_fusion = bf16[640,1536]{1,0:T(8,128)(2,1)S(1)} fusion(s32[2048]{0:T(1024)S(1)} %bitcast.35, bf16[2048,1536]{1,0:T(8,128)(2,1)} %all-gather.8.cloned.1.call-done, bf16[]{:T(256)} %constant.48.clone.1), kind=kCustom, calls=%fused_computation.36 | custom fusion | bytes 1966592 | tf_op jit(solution)/shard_map/scatter | solution.py:129
  312.8 8.5 %convolution_convert_fusion.1 = bf16[640,2048]{1,0:T(8,128)(2,1)} fusion(bf16[1536,2048]{1,0:T(8,128)(2,1)} %param.22, bf16[640,1536]{1,0:T(8,128)(2,1)S(1)} %scatter_custom_fusion, f32[1536]{0:T(1024)S(1)} %convert_element_type.85), kind=kOutput, calls=%fused_computation.28 | convolution fusion | flops 4030791680 | bytes 10885120 | tf_op jit(solution)/shard_map/dot_general | solution.py:135
  321.2 8.2 %convolution_convert_fusion.2 = bf16[640,2048]{1,0:T(8,128)(2,1)} fusion(bf16[1536,2048]{1,0:T(8,128)(2,1)} %param.21, bf16[640,1536]{1,0:T(8,128)(2,1)S(1)} %scatter_custom_fusion, f32[1536]{0:T(1024)S(1)} %convert_element_type.85), kind=kOutput, calls=%fused_computation.29 | convolution fusion | flops 4030791680 | bytes 10885120 | tf_op jit(solution)/shard_map/dot_general | solution.py:134
  329.5 0.0 copy-start.8
  329.5 0.0 all-reduce.5.cloned.1.call-update
  329.5 0.0 reduce-scatter.5.cloned.1.call-start
  329.6 8.0 %scatter_custom_fusion.1 = s32[640]{0:T(1024)S(1)} fusion(s32[2048]{0:T(1024)S(1)} %bitcast.36, s32[2048]{0:T(1024)S(1)} %get-tuple-element.40, s32[]{:T(128)} %constant.22.clone.1), kind=kCustom, calls=%fused_computation.54 | custom fusion | bytes 2564 | tf_op jit(solution)/shard_map/scatter | solution.py:23
  337.7 0.5 fusion.17
  338.1 0.0 copy-done.8
  338.1 0.6 fusion.23
  338.7 19.9 %all-reduce.1 = (bf16[640]{0:T(1024)(128)(2,1)S(1)}, bf16[640,8]{0,1:T(8,128)(2,1)S(1)}) all-reduce(bf16[640]{0:T(1024)(128)(2,1)S(1)} %fusion.17, bf16[640,8]{0,1:T(8,128)(2,1)S(1)} %fusion.23), channel_id=1, replica_groups=mesh['groups'=2,'wide'=4,'ctx'=4] {'wide'}, use_global_device_ids=true, to_apply=%region_9.10 | all-reduce | flops 5760 | bytes 23040 | tf_op jit(solution)/shard_map/psum | solution.py:140
  358.7 160.5 %all-reduce.5.cloned.1.call-done = (bf16[640,2048]{1,0:T(8,128)(2,1)}, bf16[640,2048]{1,0:T(8,128)(2,1)}) async-done(((bf16[640,2048]{1,0:T(8,128)(2,1)}, bf16[640,2048]{1,0:T(8,128)(2,1)}), (bf16[640,2048]{1,0:T(8,128)(2,1)}, bf16[640,2048]{1,0:T(8,128)(2,1)})) %all-reduce.5.cloned.1.call-update) | async-done | bytes 5242896 | tf_op jit(solution)/shard_map/psum | solution.py:139
  519.2 9.2 %fusion.18 = bf16[640,1536]{1,0:T(8,128)(2,1)S(1)} fusion(bf16[2048,1536]{1,0:T(8,128)(2,1)} %param.23, bf16[640,2048]{1,0:T(8,128)(2,1)} %get-tuple-element.44, bf16[640,2048]{1,0:T(8,128)(2,1)} %get-tuple-element.45, f32[640]{0:T(1024)S(1)} %divide_reduce_fusion, f32[640]{0:T(1024)S(1)} %add_rsqrt_fusion), kind=kOutput, calls=%fused_computation.33 | convolution fusion | flops 4040949760 | bytes 13505536 | tf_op jit(solution)/shard_map/dot_general | solution.py:144
  528.4 0.1 concatenate.3
  528.5 10.1 %gather_fusion = bf16[2048,1536]{1,0:T(8,128)(2,1)} fusion(bf16[641,1536]{1,0:T(8,128)(2,1)S(1)} %concatenate.3, s32[2048]{0:T(1024)S(1)} %broadcast_clamp_fusion), kind=kCustom, calls=%fused_computation | custom fusion | bytes 12591104 | tf_op jit(solution)/shard_map/jit(_take)/gather | solution.py:147
  538.7 6.6 %select_convert_fusion = bf16[2048,1536]{1,0:T(8,128)(2,1)} fusion(bf16[2048,1536]{1,0:T(8,128)(2,1)} %gather_fusion, pred[2048]{0:T(1024)(128)(4,1)S(1)} %compare_and_fusion), kind=kLoop, calls=%fused_computation.21 | loop fusion | flops 3145728 | bytes 12584960 | tf_op jit(solution)/shard_map/convert_element_type | solution.py:147
  545.3 0.0 copy-start.2
  545.3 0.0 copy-start.1
  545.3 0.0 reduce-scatter.5.cloned.1.call-update
  545.3 58.0 %reduce-scatter.5.cloned.1.call-done = bf16[512,1536]{1,0:T(8,128)(2,1)} async-done(((bf16[2048,1536]{1,0:T(8,128)(2,1)}), bf16[512,1536]{1,0:T(8,128)(2,1)}) %reduce-scatter.5.cloned.1.call-update) | async-done | bytes 1572880 | tf_op jit(solution)/shard_map/reduce_scatter | solution.py:146
  603.2 0.0 copy-done.2
  603.2 2.9 add_convert_fusion
  606.2 0.0 copy-done.1
  (10 shorter events, 0.1 us)
Async XLA Ops:
  6.5 1.2 copy-start
  6.5 21.8 %all-gather.4.cloned.1.call-start = ((), (), s32[]{:S(2)}) async-start(), calls=%async_computation.2 | async-start | bytes 1310720 | tf_op jit(solution)/shard_map/all_gather | solution.py:78
  8.5 38.1 %all-gather.6.cloned.1.call-start = ((), (), s32[]{:S(2)}) async-start(), calls=%async_computation.3 | async-start | bytes 1310720 | tf_op jit(solution)/shard_map/all_gather | solution.py:79
  10.3 241.0 %reduce-scatter.3.cloned.1.call-start = ((), (), s32[]{:S(2)}) async-start(), calls=%async_computation.4 | async-start | bytes 7864320 | tf_op jit(solution)/shard_map/reduce_scatter | solution.py:117
  72.4 22.0 %copy-start.4 = (bf16[2048,256]{1,0:T(8,128)(2,1)S(1)}, bf16[2048,256]{1,0:T(8,128)(2,1)}, u32[]{:S(2)}) copy-start(bf16[2048,256]{1,0:T(8,128)(2,1)} %get-tuple-element.22) | copy-start | bytes 3145732 | tf_op jit(solution)/shard_map/cond
  140.3 111.0 %copy-start.3 = (bf16[512,1536]{1,0:T(8,128)(2,1)S(1)}, bf16[512,1536]{1,0:T(8,128)(2,1)}, u32[]{:S(2)}) copy-start(bf16[512,1536]{1,0:T(8,128)(2,1)} %param.17) | copy-start | bytes 4718596
  140.4 113.9 %copy-start.7 = (bf16[1536]{0:T(1024)(128)(2,1)S(1)}, bf16[1536]{0:T(1024)(128)(2,1)}, u32[]{:S(2)}) copy-start(bf16[1536]{0:T(1024)(128)(2,1)} %param.19) | copy-start | bytes 9220
  140.4 114.0 %copy-start.5 = (s32[2048,2]{0,1:T(2,128)S(1)}, s32[2048,2]{0,1:T(2,128)}, u32[]{:S(2)}) copy-start(s32[2048,2]{0,1:T(2,128)} %param.24) | copy-start | bytes 49156
  140.4 114.0 %copy-start.6 = (s32[2048,2]{0,1:T(2,128)S(1)}, s32[2048,2]{0,1:T(2,128)}, u32[]{:S(2)}) copy-start(s32[2048,2]{0,1:T(2,128)} %param.25) | copy-start | bytes 49156
  140.4 160.9 %all-gather.8.cloned.1.call-start = ((), (), s32[]{:S(2)}) async-start(), calls=%async_computation.5 | async-start | bytes 7864320 | tf_op jit(solution)/shard_map/all_gather | solution.py:129
  254.3 264.9 %all-reduce.5.cloned.1.call-start = ((), (), s32[]{:S(2)}) async-start(), calls=%async_computation.7 | async-start | bytes 10485760 | tf_op jit(solution)/shard_map/psum | solution.py:139
  329.5 8.6 %copy-start.8 = (bf16[1536,8]{0,1:T(8,128)(2,1)S(1)}, bf16[1536,8]{0,1:T(8,128)(2,1)}, u32[]{:S(2)}) copy-start(bf16[1536,8]{0,1:T(8,128)(2,1)} %param.20) | copy-start | bytes 73732
  329.5 273.7 %reduce-scatter.5.cloned.1.call-start = ((), (), s32[]{:S(2)}) async-start(), calls=%async_computation.6 | async-start | bytes 7864320 | tf_op jit(solution)/shard_map/reduce_scatter | solution.py:146
  545.3 58.0 %copy-start.2 = (bf16[512,1536]{1,0:T(8,128)(2,1)S(1)}, bf16[512,1536]{1,0:T(8,128)(2,1)}, u32[]{:S(2)}) copy-start(bf16[512,1536]{1,0:T(8,128)(2,1)} %add_convert_fusion.1) | copy-start | bytes 4718596
  545.3 60.9 %copy-start.1 = (bf16[512,1024]{1,0:T(8,128)(2,1)S(1)}, bf16[512,1024]{1,0:T(8,128)(2,1)}, u32[]{:S(2)}) copy-start(bf16[512,1024]{1,0:T(8,128)(2,1)} %param.15) | copy-start | bytes 3145732
Sparse Core Ops, SparseCore 0:
  8.9 19.4 all-gather.3
  29.9 16.6 all-gather.5
  140.5 110.7 reduce-scatter.2
  254.4 46.8 all-gather.7
  329.6 189.4 all-reduce.4
  545.4 57.7 reduce-scatter.4
where the time goes:
time: 614 us; the launch traced here: 613 us
  waiting for transfers between devices  413 us (67%)
  matrix products  87.4 us (14%)
  local copies, waits for them, and re-layouts  41.1 us (7%)
  other arithmetic  38.2 us (6%)
  blocking collectives  19.9 us (3%)
  between operations  13.6 us (2%)
    psum x1, waiting for transfers between devices, local(): lax.psum(up_part.astype(jnp.bfloat16), 'wide').astype(jnp.float32)  160 us
    reduce_scatter x1, waiting for transfers between devices, local(): lax.psum_scatter(partial_out.astype(jnp.bfloat16), 'wide', scatter_dimens...  111 us
    reduce_scatter x1, waiting for transfers between devices, local(): lax.psum_scatter(jnp.take(expert_pad, slot_of_token, axis=0).astype(jnp.b...  58 us
    all_gather x1, waiting for transfers between devices, local(): lax.all_gather(resid, 'ctx', axis=0, tiled=True)  46.9 us
    dot_general x1, matrix products, update(): jnp.einsum('kqsr,rkd->kqsd', weights.astype(jnp.bfloat16), value_piece, p...  24 us
    reduce_sum x1, other arithmetic, update(): new_sum = running_sum * decay + jnp.sum(weights, axis=-1)  22 us
    dot_general x1, matrix products, update(): jnp.einsum('skqd,rkd->kqsr', query_blocks, key_piece, preferred_element_t...  21.1 us
    psum x1, blocking collectives, local(): lax.psum(square_part.astype(jnp.bfloat16), 'wide').astype(jnp.float32)  19.9 us
  transfers between devices with their start and end apart: 6, of which 6 were waited for; matrix products, arithmetic and copies ran while one was open for 2% of the time, Pallas kernels for 0%

commit v1 on v0

--- a/solution.py
+++ b/solution.py
@@ -10,6 +10,28 @@
 HEAD_SIZE = 128
 NEG_FILL = -1e30
 EPSILON = 1e-05
+
+
+def in_order(blocks, dim):
+    blocks = jnp.moveaxis(blocks, 0, dim)
+    dims = blocks.shape
+    return blocks.reshape(*dims[:dim], dims[dim] * dims[dim + 1], *dims[dim + 2 :])
+
+
+def ring_gather(value, axis, dim):
+    size = lax.axis_size(axis)
+    pairs = [(i, (i + 1) % size) for i in range(size)]
+    back = [(b, a) for a, b in pairs]
+    lower, upper = ([], [])
+    for step in range(size - 1):
+        if step % 2 == 0:
+            lower.append(lax.ppermute(lower[-1] if lower else value, axis, pairs))
+        else:
+            upper.append(lax.ppermute(upper[-1] if upper else value, axis, back))
+    tiles = jnp.stack([*lower[::-1], value, *upper])
+    shift = lax.axis_index(axis) - len(lower)
+    tiles = tiles[(jnp.arange(size) - shift) % size]
+    return in_order(tiles, dim)
 
 
 def token_slots(expert_ids, slot_ids, capacity):
@@ -126,7 +148,7 @@
     buffer = (
         jnp.zeros((capacity, width_local), jnp.bfloat16)
         .at[slot_of_token]
-        .set(lax.all_gather(resid, "ctx", axis=0, tiled=True), mode="drop")
+        .set(ring_gather(resid, "ctx", 0), mode="drop")
     )
     buffer_wide = buffer.astype(jnp.float32)
     square_part = jnp.sum(buffer_wide * buffer_wide, axis=1)

time: 614 us -> 635 us (1.034)
  waiting for transfers between devices: 413 us -> 421 us
  local copies, waits for them, and re-layouts: 41.1 us -> 47.5 us
    ppermute x0 -> x3, waiting for transfers between devices: none -> 53.3 us  [the longest x2 52.8 us: ring_gather(): lower.append(lax.ppermute(lower[-1] if lower else value, axis, pairs))]
    all_gather x1 -> x0, waiting for transfers between devices: 46.9 us -> none  [local(): lax.all_gather(resid, 'ctx', axis=0, tiled=True)]
    gather x0 -> x1, local copies, waits for them, and re-layouts: none -> 6.4 us  [ring_gather(): tiles = tiles[(jnp.arange(size) - shift) % size]]
  transfers between devices with their start and end apart: 6 -> 8, of which waited for: 6 -> 8; matrix products, arithmetic and copies ran while one was open for 2% -> 2% of each run, Pallas kernels for 0% -> 0%
where the time goes in v1:
time: 635 us; the launch traced here: 634 us
  waiting for transfers between devices  421 us (66%)
  matrix products  87.4 us (14%)
  local copies, waits for them, and re-layouts  47.5 us (7%)
  other arithmetic  43.4 us (7%)
  blocking collectives  18.9 us (3%)
  between operations  13.3 us (2%)
    psum x1, waiting for transfers between devices, local(): lax.psum(up_part.astype(jnp.bfloat16), 'wide').astype(jnp.float32)  163 us
    reduce_scatter x1, waiting for transfers between devices, local(): lax.psum_scatter(partial_out.astype(jnp.bfloat16), 'wide', scatter_dimens...  111 us
    reduce_scatter x1, waiting for transfers between devices, local(): lax.psum_scatter(jnp.take(expert_pad, slot_of_token, axis=0).astype(jnp.b...  58 us
    ppermute x2, waiting for transfers between devices, ring_gather(): lower.append(lax.ppermute(lower[-1] if lower else value, axis, pairs))  52.8 us
    dot_general x1, matrix products, update(): jnp.einsum('kqsr,rkd->kqsd', weights.astype(jnp.bfloat16), value_piece, p...  24 us
    reduce_sum x1, other arithmetic, update(): new_sum = running_sum * decay + jnp.sum(weights, axis=-1)  22 us
    dot_general x1, matrix products, update(): jnp.einsum('skqd,rkd->kqsr', query_blocks, key_piece, preferred_element_t...  21.1 us
    psum x1, blocking collectives, local(): lax.psum(square_part.astype(jnp.bfloat16), 'wide').astype(jnp.float32)  18.9 us
  transfers between devices with their start and end apart: 8, of which 8 were waited for; matrix products, arithmetic and copies ran while one was open for 2% of the time, Pallas kernels for 0%

profile of v1, /device:TPU:0, one launch (start us, length us, event | category | flops | bytes accessed | tf_op | source)
XLA Modules:
  0.0 634.0 jit_solution(18048706070831572900)
XLA Ops:
  6.5 0.0 copy-start
  6.5 0.0 all-gather.3.cloned.1.call-start
  6.5 1.2 copy-done
  7.8 0.7 constant_dynamic-slice_fusion.1
  8.5 0.0 all-gather.3.cloned.1.call-update
  8.5 0.0 all-gather.5.cloned.1.call-start
  8.6 1.7 constant_dynamic-slice_fusion
  10.2 0.0 all-gather.5.cloned.1.call-update
  10.3 0.0 reduce-scatter.3.cloned.1.call-start
  10.3 18.0 %all-gather.3.cloned.1.call-done = bf16[2048,256]{1,0:T(8,128)(2,1)} async-done(((bf16[512,256]{1,0:T(8,128)(2,1)}), bf16[2048,256]{1,0:T(8,128)(2,1)}) %all-gather.3.cloned.1.call-update) | async-done | bytes 1048592 | tf_op jit(solution)/shard_map/all_gather | solution.py:100
  28.3 18.3 %all-gather.5.cloned.1.call-done = bf16[2048,256]{1,0:T(8,128)(2,1)} async-done(((bf16[512,256]{1,0:T(8,128)(2,1)}), bf16[2048,256]{1,0:T(8,128)(2,1)}) %all-gather.5.cloned.1.call-update) | async-done | bytes 1048592 | tf_op jit(solution)/shard_map/all_gather | solution.py:101
  46.6 75.7 %conditional.1 = (f32[2,6,512]{2,1,0:T(8,128)S(1)}, f32[2,6,512,128]{2,3,1,0:T(8,128)}) conditional(s32[]{:T(128)} %convert_element_type.76, (s32[]{:T(128)}, s32[512]{0:T(512)S(1)}, bf16[2048,256]{1,0:T(8,128)(2,1)}, bf16[512,1536]{1,0:T(8,128)(2,1)}, bf16[2048,256]{1,0:T(8,128)(2,1)}) %tuple.13, () %tuple.14), branch_computations={%region_0.3_spmd, %region_3.4_spmd} | conditional | flops 6607870464 | bytes 180058160 | solution.py:129
  46.6 0.8 iota_compare_fusion
  47.5 1.7 copy.28
  49.2 2.1 reshape.122
  51.3 21.1 %fusion = (f32[2,6,512]{2,1,0:T(8,128)S(1)}, f32[2,2048,512,6]{2,1,3,0:T(8,128)}) fusion(pred[512,2048]{0,1:T(8,128)(4,1)S(1)} %iota_compare_fusion, bf16[512,2,6,128]{0,3,2,1:T(8,128)(2,1)S(1)} %bitcast.37, bf16[2048,2,128,1]{2,1,0,3:T(2,128)(2,1)} %bitcast.39), kind=kOutput, calls=%fused_computation.6 | convolution fusion | flops 3258968064 | bytes 54026240 | tf_op jit(solution)/shard_map/cond/branch_0_fun/skqd,rkd->kqsr/dot_general | solution.py:109
  72.4 0.0 copy-start.4
  72.4 22.0 %fusion.2 = f32[2,6,512]{2,1,0:T(8,128)S(1)} fusion(f32[2,2048,512,6]{2,1,3,0:T(8,128)} %get-tuple-element.49, f32[2,6,512]{2,1,0:T(8,128)S(1)} %get-tuple-element.48, pred[512,2048]{0,1:T(8,128)(4,1)S(1)} %iota_compare_fusion), kind=kLoop, calls=%fused_computation.8 | loop fusion | flops 62908416 | bytes 51429376 | tf_op jit(solution)/shard_map/cond/branch_0_fun/reduce_sum | solution.py:120
  94.4 0.0 copy-done.4
  94.4 0.3 reshape.124
  94.7 24.0 %fusion.6 = f32[2,6,512,128]{3,2,1,0:T(8,128)} fusion(f32[2,2048,512,6]{2,1,3,0:T(8,128)} %get-tuple-element.49, f32[2,6,512]{2,1,0:T(8,128)S(1)} %get-tuple-element.48, pred[512,2048]{0,1:T(8,128)(4,1)S(1)} %iota_compare_fusion, f32[2,6,512]{2,1,0:T(8,128)S(1)} %get-tuple-element.46, bf16[2048,2,128,1]{2,1,0,3:T(2,128)(2,1)S(1)} %bitcast.41), kind=kOutput, calls=%fused_computation.12 | convolution fusion | flops 3284926464 | bytes 55623680 | tf_op jit(solution)/shard_map/cond/branch_0_fun/kqsr,rkd->kqsd/dot_general | solution.py:121
  118.8 3.5 copy.38
  122.3 2.3 divide_convert_fusion
  124.7 15.7 %convolution_convert_fusion = bf16[512,6144]{1,0:T(8,128)(2,1)} fusion(bf16[512,1536]{0,1:T(8,128)(2,1)S(1)} %bitcast.40, bf16[1536,6144]{1,0:T(8,128)(2,1)} %param.18), kind=kOutput, calls=%fused_computation.23 | convolution fusion | flops 9666822144 | bytes 26738688 | tf_op jit(solution)/shard_map/dot_general | solution.py:138
  140.3 0.0 copy-start.7
  140.3 0.0 copy-start.5
  140.4 0.0 reduce-scatter.3.cloned.1.call-update
  140.4 0.0 all-reduce.5.cloned.1.call-start
  140.4 110.9 %reduce-scatter.3.cloned.1.call-done = bf16[512,1536]{1,0:T(8,128)(2,1)} async-done(((bf16[512,6144]{1,0:T(8,128)(2,1)}), bf16[512,1536]{1,0:T(8,128)(2,1)}) %reduce-scatter.3.cloned.1.call-update) | async-done | bytes 1572880 | tf_op jit(solution)/shard_map/reduce_scatter | solution.py:139
  251.3 2.3 add_convert_fusion.1
  253.6 0.0 copy-start.2
  253.6 0.1 collective-permute-start
  253.7 1.7 collective-permute-start.2
  255.4 33.3 %collective-permute-done = bf16[512,1536]{1,0:T(8,128)(2,1)} collective-permute-done((bf16[512,1536]{1,0:T(8,128)(2,1)S(1)}, bf16[512,1536]{1,0:T(8,128)(2,1)}, u32[]{:S(2)}, u32[]{:S(2)}) %collective-permute-start) | collective-permute-done | bytes 1572896 | tf_op jit(solution)/shard_map/ppermute | solution.py:28
  288.7 0.0 collective-permute-start.1
  288.7 0.0 copy-done.7
  288.7 0.0 copy-done.5
  288.7 0.0 copy-done.6
  288.7 0.1 fusion.35
  288.8 0.5 collective-permute-done.2
  289.3 19.5 %collective-permute-done.1 = bf16[512,1536]{1,0:T(8,128)(2,1)} collective-permute-done((bf16[512,1536]{1,0:T(8,128)(2,1)}, bf16[512,1536]{1,0:T(8,128)(2,1)}, u32[]{:S(2)}, u32[]{:S(2)}) %collective-permute-start.1) | collective-permute-done | bytes 1572896 | tf_op jit(solution)/shard_map/ppermute | solution.py:28
  308.8 5.9 pad_maximum_fusion
  314.8 0.0 copy-done.2
  314.8 6.4 %gather_fusion = bf16[4,512,1536]{2,1,0:T(8,128)(2,1)} fusion(bf16[4,512,1536]{2,1,0:T(8,128)(2,1)} %pad_maximum_fusion, s32[1024]{0:T(1024)S(1)} %pad_clamp_fusion), kind=kCustom, calls=%fused_computation | custom fusion | bytes 12582928 | tf_op jit(solution)/shard_map/gather | solution.py:33
  321.2 11.4 %scatter_custom_fusion = bf16[640,1536]{1,0:T(8,128)(2,1)S(1)} fusion(s32[2048]{0:T(1024)S(1)} %bitcast.44, bf16[2048,1536]{1,0:T(8,128)(2,1)} %bitcast.38, bf16[]{:T(256)} %constant.60.clone.1), kind=kCustom, calls=%fused_computation.38 | custom fusion | bytes 1966592 | tf_op jit(solution)/shard_map/scatter | solution.py:151
  332.6 8.5 %convolution_convert_fusion.1 = bf16[640,2048]{1,0:T(8,128)(2,1)} fusion(bf16[1536,2048]{1,0:T(8,128)(2,1)} %param.22, bf16[640,1536]{1,0:T(8,128)(2,1)S(1)} %scatter_custom_fusion, f32[1536]{0:T(1024)S(1)} %convert_element_type.85), kind=kOutput, calls=%fused_computation.30 | convolution fusion | flops 4030791680 | bytes 10885120 | tf_op jit(solution)/shard_map/dot_general | solution.py:157
  341.1 8.2 %convolution_convert_fusion.2 = bf16[640,2048]{1,0:T(8,128)(2,1)} fusion(bf16[1536,2048]{1,0:T(8,128)(2,1)} %param.21, bf16[640,1536]{1,0:T(8,128)(2,1)S(1)} %scatter_custom_fusion, f32[1536]{0:T(1024)S(1)} %convert_element_type.85), kind=kOutput, calls=%fused_computation.31 | convolution fusion | flops 4030791680 | bytes 10885120 | tf_op jit(solution)/shard_map/dot_general | solution.py:156
  349.4 0.0 all-reduce.5.cloned.1.call-update
  349.4 0.0 reduce-scatter.5.cloned.1.call-start
  349.4 8.0 %scatter_custom_fusion.1 = s32[640]{0:T(1024)S(1)} fusion(s32[2048]{0:T(1024)S(1)} %bitcast.45, s32[2048]{0:T(1024)S(1)} %get-tuple-element.40, s32[]{:T(128)} %constant.36.clone.1), kind=kCustom, calls=%fused_computation.60 | custom fusion | bytes 2564 | tf_op jit(solution)/shard_map/scatter | solution.py:45
  357.5 0.5 fusion.17
  358.0 0.0 copy-done.8
  358.0 0.6 fusion.23
  358.6 18.9 %all-reduce.1 = (bf16[640]{0:T(1024)(128)(2,1)S(1)}, bf16[640,8]{0,1:T(8,128)(2,1)S(1)}) all-reduce(bf16[640]{0:T(1024)(128)(2,1)S(1)} %fusion.17, bf16[640,8]{0,1:T(8,128)(2,1)S(1)} %fusion.23), channel_id=1, replica_groups=mesh['groups'=2,'wide'=4,'ctx'=4] {'wide'}, use_global_device_ids=true, to_apply=%region_9.10 | all-reduce | flops 5760 | bytes 23040 | tf_op jit(solution)/shard_map/psum | solution.py:162
  377.6 162.9 %all-reduce.5.cloned.1.call-done = (bf16[640,2048]{1,0:T(8,128)(2,1)}, bf16[640,2048]{1,0:T(8,128)(2,1)}) async-done(((bf16[640,2048]{1,0:T(8,128)(2,1)}, bf16[640,2048]{1,0:T(8,128)(2,1)}), (bf16[640,2048]{1,0:T(8,128)(2,1)}, bf16[640,2048]{1,0:T(8,128)(2,1)})) %all-reduce.5.cloned.1.call-update) | async-done | bytes 5242896 | tf_op jit(solution)/shard_map/psum | solution.py:161
  540.5 9.2 %fusion.18 = bf16[640,1536]{1,0:T(8,128)(2,1)S(1)} fusion(bf16[2048,1536]{1,0:T(8,128)(2,1)} %param.23, bf16[640,2048]{1,0:T(8,128)(2,1)} %get-tuple-element.44, bf16[640,2048]{1,0:T(8,128)(2,1)} %get-tuple-element.45, f32[640]{0:T(1024)S(1)} %divide_reduce_fusion, f32[640]{0:T(1024)S(1)} %add_rsqrt_fusion), kind=kOutput, calls=%fused_computation.35 | convolution fusion | flops 4040949760 | bytes 13505536 | tf_op jit(solution)/shard_map/dot_general | solution.py:166
  549.7 0.1 concatenate.3
  549.8 10.1 %gather_fusion.1 = bf16[2048,1536]{1,0:T(8,128)(2,1)} fusion(bf16[641,1536]{1,0:T(8,128)(2,1)S(1)} %concatenate.3, s32[2048]{0:T(1024)S(1)} %broadcast_clamp_fusion), kind=kCustom, calls=%fused_computation.1 | custom fusion | bytes 12591104 | tf_op jit(solution)/shard_map/jit(_take)/gather | solution.py:169
  560.0 6.6 %select_convert_fusion = bf16[2048,1536]{1,0:T(8,128)(2,1)} fusion(bf16[2048,1536]{1,0:T(8,128)(2,1)} %gather_fusion.1, pred[2048]{0:T(1024)(128)(4,1)S(1)} %compare_and_fusion), kind=kLoop, calls=%fused_computation.22 | loop fusion | flops 3145728 | bytes 12584960 | tf_op jit(solution)/shard_map/convert_element_type | solution.py:169
  566.5 0.0 reduce-scatter.5.cloned.1.call-update
  566.6 58.0 %reduce-scatter.5.cloned.1.call-done = bf16[512,1536]{1,0:T(8,128)(2,1)} async-done(((bf16[2048,1536]{1,0:T(8,128)(2,1)}), bf16[512,1536]{1,0:T(8,128)(2,1)}) %reduce-scatter.5.cloned.1.call-update) | async-done | bytes 1572880 | tf_op jit(solution)/shard_map/reduce_scatter | solution.py:168
  624.5 0.0 copy-done.3
  624.5 2.9 add_convert_fusion
  627.5 0.0 copy-done.1
  (16 shorter events, 0.1 us)
Async XLA Ops:
  6.5 1.2 copy-start
  6.5 21.8 %all-gather.3.cloned.1.call-start = ((), (), s32[]{:S(2)}) async-start(), calls=%async_computation.2 | async-start | bytes 1310720 | tf_op jit(solution)/shard_map/all_gather | solution.py:100
  8.5 38.1 %all-gather.5.cloned.1.call-start = ((), (), s32[]{:S(2)}) async-start(), calls=%async_computation.3 | async-start | bytes 1310720 | tf_op jit(solution)/shard_map/all_gather | solution.py:101
  10.3 241.0 %reduce-scatter.3.cloned.1.call-start = ((), (), s32[]{:S(2)}) async-start(), calls=%async_computation.4 | async-start | bytes 7864320 | tf_op jit(solution)/shard_map/reduce_scatter | solution.py:139
  72.4 22.0 %copy-start.4 = (bf16[2048,256]{1,0:T(8,128)(2,1)S(1)}, bf16[2048,256]{1,0:T(8,128)(2,1)}, u32[]{:S(2)}) copy-start(bf16[2048,256]{1,0:T(8,128)(2,1)} %get-tuple-element.22) | copy-start | bytes 3145732 | tf_op jit(solution)/shard_map/cond
  140.3 148.3 %copy-start.7 = (bf16[1536]{0:T(1024)(128)(2,1)S(1)}, bf16[1536]{0:T(1024)(128)(2,1)}, u32[]{:S(2)}) copy-start(bf16[1536]{0:T(1024)(128)(2,1)} %param.19) | copy-start | bytes 9220
  140.3 148.4 %copy-start.5 = (s32[2048,2]{0,1:T(2,128)S(1)}, s32[2048,2]{0,1:T(2,128)}, u32[]{:S(2)}) copy-start(s32[2048,2]{0,1:T(2,128)} %param.24) | copy-start | bytes 49156
  140.4 148.4 %copy-start.6 = (s32[2048,2]{0,1:T(2,128)S(1)}, s32[2048,2]{0,1:T(2,128)}, u32[]{:S(2)}) copy-start(s32[2048,2]{0,1:T(2,128)} %param.25) | copy-start | bytes 49156
  140.4 400.1 %all-reduce.5.cloned.1.call-start = ((), (), s32[]{:S(2)}) async-start(), calls=%async_computation.6 | async-start | bytes 10485760 | tf_op jit(solution)/shard_map/psum | solution.py:161
  253.6 61.2 %copy-start.2 = (bf16[512,1536]{1,0:T(8,128)(2,1)}, bf16[512,1536]{1,0:T(8,128)(2,1)S(1)}, u32[]{:S(2)}) copy-start(bf16[512,1536]{1,0:T(8,128)(2,1)S(1)} %add_convert_fusion.1) | copy-start | bytes 4718596
  253.6 35.1 %collective-permute-start = (bf16[512,1536]{1,0:T(8,128)(2,1)S(1)}, bf16[512,1536]{1,0:T(8,128)(2,1)}, u32[]{:S(2)}, u32[]{:S(2)}) collective-permute-start(bf16[512,1536]{1,0:T(8,128)(2,1)S(1)} %add_convert_fusion.1), channel_id=1, source_target_pairs={{0,1},{1,2},{2,3},{3,0},{4,5},{5,6},{6,7},{7,4},{8,9},{9,10},{10,1... | collective-permute-start | bytes 4718600 | tf_op jit(solution)/shard_map/ppermute | solution.py:28
  253.7 35.7 %collective-permute-start.2 = (bf16[512,1536]{1,0:T(8,128)(2,1)S(1)}, bf16[512,1536]{1,0:T(8,128)(2,1)}, u32[]{:S(2)}, u32[]{:S(2)}) collective-permute-start(bf16[512,1536]{1,0:T(8,128)(2,1)S(1)} %add_convert_fusion.1), channel_id=1, source_target_pairs={{1,0},{2,1},{3,2},{0,3},{5,4},{6,5},{7,6},{4,7},{9,8},{10,9},{11,1... | collective-permute-start | bytes 4718600 | tf_op jit(solution)/shard_map/ppermute | solution.py:30
  288.7 20.2 %collective-permute-start.1 = (bf16[512,1536]{1,0:T(8,128)(2,1)}, bf16[512,1536]{1,0:T(8,128)(2,1)}, u32[]{:S(2)}, u32[]{:S(2)}) collective-permute-start(bf16[512,1536]{1,0:T(8,128)(2,1)} %collective-permute-done), channel_id=1, source_target_pairs={{0,1},{1,2},{2,3},{3,0},{4,5},{5,6},{6,7},{7,4},{8,9},{9,10},{10,1... | collective-permute-start | bytes 4718600 | tf_op jit(solution)/shard_map/ppermute | solution.py:28
  349.4 8.6 %copy-start.8 = (bf16[1536,8]{0,1:T(8,128)(2,1)S(1)}, bf16[1536,8]{0,1:T(8,128)(2,1)}, u32[]{:S(2)}) copy-start(bf16[1536,8]{0,1:T(8,128)(2,1)} %param.20) | copy-start | bytes 73732
  349.4 275.2 %reduce-scatter.5.cloned.1.call-start = ((), (), s32[]{:S(2)}) async-start(), calls=%async_computation.5 | async-start | bytes 7864320 | tf_op jit(solution)/shard_map/reduce_scatter | solution.py:168
  566.5 58.0 %copy-start.3 = (bf16[512,1536]{1,0:T(8,128)(2,1)S(1)}, bf16[512,1536]{1,0:T(8,128)(2,1)}, u32[]{:S(2)}) copy-start(bf16[512,1536]{1,0:T(8,128)(2,1)} %copy-done.2) | copy-start | bytes 4718596
  566.5 60.9 %copy-start.1 = (bf16[512,1024]{1,0:T(8,128)(2,1)S(1)}, bf16[512,1024]{1,0:T(8,128)(2,1)}, u32[]{:S(2)}) copy-start(bf16[512,1024]{1,0:T(8,128)(2,1)} %param.15) | copy-start | bytes 3145732
Sparse Core Ops, SparseCore 0:
  8.9 19.4 all-gather.2
  29.9 16.6 all-gather.4
  140.5 110.7 reduce-scatter.2
  349.5 190.9 all-reduce.4
  566.7 57.7 reduce-scatter.4
